TPU v7x, 256 devices: a whole 4x4x8 slice. The times are simulated.
256 devices in a mesh: dp: 16 (over z_lo, x, core), fsdp: 16 (over y, z_hi).
Axes of the slice: x: 4, y: 4, z: 8 (z_hi: 4, z_lo: 2; z = z_hi * 2 + z_lo), core: 2. Of those that a mesh axis runs over, the one named last changes fastest.
Arguments:
- hidden_in: bfloat16 [131072, 1536], P(('dp', 'fsdp')), may hold values from -6 to 6
- grad_out: bfloat16 [131072, 1536], P(('dp', 'fsdp')), may hold values from -6 to 6
- lengths: int32 [256, 3], P(('dp', 'fsdp')), may hold values from 1 to 510, as said below
- conv_kernel: float32 [5, 1536], replicated, may hold values from -3 to 3
- norm_gain: float32 [1536], replicated, may hold values from 0.5 to 2
- out_weight: bfloat16 [1536, 1536], P('fsdp'), may hold values from -0.15625 to 0.15625
Outputs:
- output: float32 [131072, 1536], P(('dp', 'fsdp'))
- grad_hidden: float32 [131072, 1536], P(('dp', 'fsdp'))
- grad_weight: float32 [1536, 1536], P('fsdp')
- grad_kernel: float32 [5, 1536], replicated
- grad_gain: float32 [1536], replicated
Inputs may be any that keep to these rules, and one draw needn't show every extreme that they name: `lengths`: each row sums to at most 512. A row whose sum exceeds (3) * 128 sums to exactly 512, holds 2 utterances of length 1 followed by one of length 510, and then the row with the same fsdp index whose dp index differs by half the dp axis sums to at most (2) * 128; every other row sums to at most (3) * 128. Some row in every draw sums to 512.
All inputs are finite; a program needn't handle non-finite values.
Results may differ from a plain program's by a relative error of at most 0.003.
Values may be sent and summed in bfloat16 or wider, within the bound.
No kernel may reach another device: no remote copies, remote signals or barrier semaphores. Data moves between devices by JAX's collectives and lax.ppermute only.
A program may use at most 128 MiB of HBM per device.

v0:
```python
import math
import jax
import jax.numpy as jnp
from jax import lax
from jax.sharding import PartitionSpec as P


def tap_mask(lengths, frames, count):
    utt_ends = jnp.cumsum(lengths)
    position = jnp.arange(frames, dtype=jnp.int32)
    segment_id = jnp.sum((position[:, None] >= utt_ends[None, :]).astype(jnp.int32), axis=1)
    inside = position < utt_ends[-1]
    half_width = count // 2
    segment_pad = jnp.pad(segment_id, half_width, constant_values=-1)
    inside_pad = jnp.pad(inside, half_width, constant_values=False)
    rows_out = []
    for k in range(count):
        same = (segment_pad[k : k + frames] == segment_id) & inside_pad[k : k + frames] & inside
        rows_out.append(same.astype(jnp.float32))
    return jnp.stack(rows_out)


def shifted(x, half_width):
    frames = x.shape[0]
    padded = jnp.pad(x, ((half_width, half_width), (0, 0)))
    return [padded[k : k + frames] for k in range(2 * half_width + 1)]


def butterfly(x, axis):
    size = lax.axis_size(axis)
    step = 1
    while step < size:
        pairs = [(i, i ^ step) for i in range(size)]
        x = x + lax.ppermute(x, axis, pairs)
        step *= 2
    return x


def shards(hidden_in, grad_out, lengths, conv_kernel, norm_gain, out_weight):
    frames, chans = hidden_in.shape
    count = conv_kernel.shape[0]
    half_width = count // 2
    full_weight = lax.all_gather(out_weight, "fsdp", axis=0, tiled=True)
    taps = tap_mask(lengths[0], frames, count)
    live = taps[half_width][:, None]
    views = shifted(hidden_in, half_width)
    mixed = jnp.zeros((frames, chans), jnp.float32)
    for k in range(count):
        mixed = mixed + conv_kernel[k] * views[k].astype(jnp.float32) * taps[k][:, None]
    centred = mixed - jnp.mean(mixed, axis=-1, keepdims=True)
    inverse = lax.rsqrt(jnp.mean(centred * centred, axis=-1, keepdims=True) + 1e-05)
    normed = centred * inverse
    scaled = normed * norm_gain
    squash = jax.nn.sigmoid(scaled)
    activation = (scaled * squash * live).astype(jnp.bfloat16)
    weight_terms = lax.dot_general(
        activation, grad_out, (((0,), (0,)), ((), ())), preferred_element_type=jnp.float32
    )
    shard_sum = lax.psum_scatter(weight_terms, "fsdp", scatter_dimension=0, tiled=True)
    output = jnp.dot(activation, full_weight, preferred_element_type=jnp.float32)
    grad_act = lax.dot_general(
        grad_out, full_weight, (((1,), (1,)), ((), ())), preferred_element_type=jnp.float32
    )
    grad_scaled = grad_act * live * squash * (1.0 + scaled * (1.0 - squash))
    gain_grad = jnp.sum(grad_scaled * normed, axis=0)
    grad_normed = grad_scaled * norm_gain
    grad_mixed = inverse * (
        grad_normed
        - jnp.mean(grad_normed, axis=-1, keepdims=True)
        - normed * jnp.mean(grad_normed * normed, axis=-1, keepdims=True)
    )
    kernel_rows = []
    for k in range(count):
        weighted = grad_mixed * taps[k][:, None]
        kernel_rows.append(jnp.sum(weighted * views[k].astype(jnp.float32), axis=0))
    back_views = shifted(grad_mixed, half_width)
    grad_hidden = jnp.zeros((frames, chans), jnp.float32)
    for k in range(count):
        grad_hidden = grad_hidden + conv_kernel[k] * (
            back_views[count - 1 - k] * taps[count - 1 - k][:, None]
        )
    small = jnp.concatenate([jnp.stack(kernel_rows), gain_grad[None]], axis=0)
    small = butterfly(small, "fsdp")
    total = butterfly(jnp.concatenate([shard_sum, small], axis=0), "dp")
    rows = shard_sum.shape[0]
    dp_count = lax.axis_size("dp")
    fsdp_count = lax.axis_size("fsdp")
    factor = 1.0 / math.sqrt(frames * dp_count * fsdp_count)
    weight_sum = total[:rows] * factor
    kernel_sum = total[rows : rows + count] * factor
    gain_sum = total[rows + count] * factor
    return (output, grad_hidden, weight_sum, kernel_sum, gain_sum)


def solution(mesh):
    placed = (
        P(("dp", "fsdp"), None),
        P(("dp", "fsdp"), None),
        P(("dp", "fsdp"), None),
        P(),
        P(),
        P("fsdp", None),
    )
    return jax.shard_map(
        shards,
        mesh=mesh,
        in_specs=placed,
        out_specs=(P(("dp", "fsdp"), None), P(("dp", "fsdp"), None), P("fsdp", None), P(), P()),
        check_vma=False,
    )
```

profile of v0, /device:TPU:2, one launch (start us, length us, event | category | flops | bytes accessed | tf_op | source)
XLA Modules:
  0.0 291.9 jit_solution(425887298165945984)
XLA Ops:
  7.2 0.0 copy-start
  7.2 0.0 all-gather.2.cloned.1.call-start
  7.2 0.7 all-gather.2.cloned.1.call-update
  7.9 0.0 reduce-scatter.2.cloned.1.call-start
  8.0 0.8 reduce-window.4
  8.8 0.6 slice.88
  9.4 0.6 iota_compare_fusion.1
  10.0 0.1 convert_reduce_fusion
  10.1 1.1 slice_reduce_fusion.4
  11.2 0.7 and_convert_fusion.4
  11.9 0.0 copy-start.6
  11.9 8.6 %fusion.28 = (f32[512]{0:T(512)S(1)}, f32[512,1536]{1,0:T(8,128)S(1)}) fusion(f32[512]{0:T(512)S(1)} %get-tuple-element.24, f32[1536]{0:T(1024)S(1)} %get-tuple-element.16, f32[512]{0:T(512)S(1)} %get-tuple-element.22, f32[1536]{0:T(1024)S(1)} %get-tuple-element.17, f32[512]{0:T(512)S(1)} %get-tuple-element.26, bf16[512,1536]{1,0:T(8,128)(2,1)} %param.6, ...), kind=kLoop, calls=%fused_computation.80 | loop fusion | flops 15728128 | bytes 4761600 | tf_op jit(solution)/shard_map/reduce_sum | solution.py:50
  20.5 0.0 copy-start.1
  20.5 0.4 multiply_reduce_fusion.2
  21.0 1.2 copy-done.1
  22.2 0.0 copy-done
  22.2 0.0 copy-done.6
  22.2 5.4 %fusion.26 = f32[1536,1536]{1,0:T(8,128)} fusion(bf16[512,1536]{1,0:T(8,128)(2,1)S(1)} %copy-done, f32[512,1536]{1,0:T(8,128)S(1)} %get-tuple-element.20, f32[1536]{0:T(1024)S(1)} %copy-done.6, f32[512]{0:T(512)S(1)} %add_rsqrt_fusion, f32[512]{0:T(512)S(1)} %broadcast_multiply_fusion.2, f32[512]{0:T(512)S(1)} %get-tuple-element.26), kind=kOutput, calls=%fused_computation.78 | convolution fusion | flops 2422996992 | bytes 14168064 | tf_op jit(solution)/shard_map/dot_general | solution.py:56
  27.6 0.0 reduce-scatter.2.cloned.1.call-update
  27.7 0.0 copy-start.5
  27.7 64.1 %all-gather.2.cloned.1.call-done = bf16[1536,1536]{1,0:T(8,128)(2,1)} async-done(((bf16[96,1536]{1,0:T(8,128)(2,1)}), bf16[1536,1536]{1,0:T(8,128)(2,1)}) %all-gather.2.cloned.1.call-update) | async-done | bytes 4718608 | tf_op jit(solution)/shard_map/all_gather | solution.py:43
  91.8 0.0 copy-start.2
  91.8 7.1 %multiply_reduce_fusion = (f32[1536]{0:T(1024)S(1)}, f32[512]{0:T(512)S(1)}, f32[512]{0:T(512)S(1)}, f32[512,1536]{1,0:T(8,128)S(1)}) fusion(f32[512,1536]{1,0:T(8,128)} %copy-done.1, f32[512]{0:T(512)S(1)} %add_rsqrt_fusion, f32[512]{0:T(512)S(1)} %broadcast_multiply_fusion.2, f32[1536]{0:T(1024)S(1)} %copy-done.6, f32[512]{0:T(512)S(1)} %get-tuple-element.26, ...), kind=kOutput, calls=%fused_computation.27 | convolution fusion | flops 2430072320 | bytes 12605440 | tf_op jit(solution)/shard_map/dot_general | solution.py:61
  99.0 0.0 copy-done.5
  99.0 0.0 copy-done.2
  99.0 5.8 %fusion.15 = (f32[1536]{0:T(1024)S(1)}, f32[1536]{0:T(1024)S(1)}, f32[1536]{0:T(1024)S(1)}, f32[1536]{0:T(1024)S(1)}, f32[1536]{0:T(1024)S(1)}, /*index=5*/f32[512,1536]{1,0:T(8,128)}) fusion(f32[512]{0:T(512)S(1)} %get-tuple-element.24, bf16[512,1536]{1,0:T(8,128)(2,1)S(1)} %copy-done.5, f32[512]{0:T(512)S(1)} %get-tuple-element.22, ...), kind=kLoop, calls=%fused_computation.26 | loop fusion | flops 21225984 | bytes 11065344 | tf_op jit(solution)/shard_map/reduce_sum | solution.py:75
  104.8 0.1 concatenate.6
  104.9 6.4 %collective-permute-start = (f32[6,1536]{1,0:T(8,128)S(1)}, f32[6,1536]{1,0:T(8,128)S(1)}, u32[]{:S(2)}, u32[]{:S(2)}) collective-permute-start(f32[6,1536]{1,0:T(8,128)S(1)} %concatenate.6), channel_id=1, source_target_pairs={{0,1},{1,0},{2,3},{3,2},{4,5},{5,4},{6,7},{7,6},{8,9},{9,8},{10,11... | collective-permute-start | bytes 110600 | tf_op jit(solution)/shard_map/ppermute | solution.py:34
  111.3 6.6 %collective-permute-done = f32[6,1536]{1,0:T(8,128)S(1)} collective-permute-done((f32[6,1536]{1,0:T(8,128)S(1)}, f32[6,1536]{1,0:T(8,128)S(1)}, u32[]{:S(2)}, u32[]{:S(2)}) %collective-permute-start) | collective-permute-done | bytes 36896 | tf_op jit(solution)/shard_map/ppermute | solution.py:34
  117.9 0.1 collective-permute-start.1
  118.0 11.7 %collective-permute-done.1 = f32[6,1536]{1,0:T(8,128)S(1)} collective-permute-done((f32[6,1536]{1,0:T(8,128)S(1)}, f32[6,1536]{1,0:T(8,128)S(1)}, u32[]{:S(2)}, u32[]{:S(2)}) %collective-permute-start.1) | collective-permute-done | bytes 36896 | tf_op jit(solution)/shard_map/ppermute | solution.py:34
  129.7 1.5 collective-permute-start.2
  131.3 3.6 %collective-permute-done.2 = f32[6,1536]{1,0:T(8,128)S(1)} collective-permute-done((f32[6,1536]{1,0:T(8,128)S(1)}, f32[6,1536]{1,0:T(8,128)S(1)}, u32[]{:S(2)}, u32[]{:S(2)}) %collective-permute-start.2) | collective-permute-done | bytes 36896 | tf_op jit(solution)/shard_map/ppermute | solution.py:34
  134.9 3.0 %collective-permute-start.3 = (f32[6,1536]{1,0:T(8,128)S(1)}, f32[6,1536]{1,0:T(8,128)S(1)}, u32[]{:S(2)}, u32[]{:S(2)}) collective-permute-start(f32[6,1536]{1,0:T(8,128)S(1)} %add.87), channel_id=1, source_target_pairs={{0,8},{1,9},{2,10},{3,11},{4,12},{5,13},{6,14},{7,15},{8,0},{9,1},... | collective-permute-start | bytes 110600 | tf_op jit(solution)/shard_map/ppermute | solution.py:34
  137.8 3.2 %collective-permute-done.3 = f32[6,1536]{1,0:T(8,128)S(1)} collective-permute-done((f32[6,1536]{1,0:T(8,128)S(1)}, f32[6,1536]{1,0:T(8,128)S(1)}, u32[]{:S(2)}, u32[]{:S(2)}) %collective-permute-start.3) | collective-permute-done | bytes 36896 | tf_op jit(solution)/shard_map/ppermute | solution.py:34
  141.0 88.5 %reduce-scatter.2.cloned.1.call-done = f32[96,1536]{1,0:T(8,128)} async-done(((f32[1536,1536]{1,0:T(8,128)}), f32[96,1536]{1,0:T(8,128)}) %reduce-scatter.2.cloned.1.call-update) | async-done | bytes 589840 | tf_op jit(solution)/shard_map/reduce_scatter | solution.py:59
  229.5 0.0 copy-start.3
  229.5 1.3 pad_maximum_fusion
  230.8 0.3 collective-permute-start.4
  231.0 2.1 collective-permute-done.4
  233.1 1.2 fusion.25
  234.3 0.5 collective-permute-start.5
  234.8 16.0 %collective-permute-done.5 = f32[102,1536]{1,0:T(8,128)S(1)} collective-permute-done((f32[102,1536]{1,0:T(8,128)S(1)}, f32[102,1536]{1,0:T(8,128)S(1)}, u32[]{:S(2)}, u32[]{:S(2)}) %collective-permute-start.5) | collective-permute-done | bytes 626720 | tf_op jit(solution)/shard_map/ppermute | solution.py:34
  250.8 0.1 add.90
  250.9 2.2 collective-permute-start.6
  253.1 0.0 copy-done.3
  253.1 0.0 copy-start.4
  253.1 7.1 %fusion.27 = f32[512,1536]{1,0:T(8,128)} fusion(bf16[1536,1536]{1,0:T(8,128)(2,1)} %all-gather.2.cloned.1.call-done, f32[512,1536]{1,0:T(8,128)S(1)} %copy-done.3, f32[1536]{0:T(1024)S(1)} %copy-done.6, f32[512]{0:T(512)S(1)} %add_rsqrt_fusion, f32[512]{0:T(512)S(1)} %broadcast_multiply_fusion.2, f32[512]{0:T(512)S(1)} %get-tuple-element.26), kind=kOutput, calls=%fused_computation.79 | convolution fusion | flops 2422996992 | bytes 11022336 | tf_op jit(solution)/shard_map/dot_general | solution.py:60
  260.1 7.9 %collective-permute-done.6 = f32[102,1536]{1,0:T(8,128)S(1)} collective-permute-done((f32[102,1536]{1,0:T(8,128)S(1)}, f32[102,1536]{1,0:T(8,128)S(1)}, u32[]{:S(2)}, u32[]{:S(2)}) %collective-permute-start.6) | collective-permute-done | bytes 626720 | tf_op jit(solution)/shard_map/ppermute | solution.py:34
  268.0 0.1 add.91
  268.1 1.1 collective-permute-start.7
  269.2 0.0 copy-done.4
  269.2 4.0 %multiply_add_fusion = f32[512,1536]{1,0:T(8,128)} fusion(f32[512,1536]{1,0:T(8,128)S(1)} %copy-done.4, f32[512]{0:T(512)S(1)} %get-tuple-element.24, f32[1536]{0:T(1024)S(1)} %get-tuple-element.16, f32[512]{0:T(512)S(1)} %get-tuple-element.22, f32[1536]{0:T(1024)S(1)} %get-tuple-element.17, f32[512]{0:T(512)S(1)} %get-tuple-element.26, ...), kind=kLoop, calls=%fused_computation.28 | loop fusion | flops 11010048 | bytes 6332416 | tf_op jit(solution)/shard_map/add | solution.py:79
  273.2 9.7 %collective-permute-done.7 = f32[102,1536]{1,0:T(8,128)S(1)} collective-permute-done((f32[102,1536]{1,0:T(8,128)S(1)}, f32[102,1536]{1,0:T(8,128)S(1)}, u32[]{:S(2)}, u32[]{:S(2)}) %collective-permute-start.7) | collective-permute-done | bytes 626720 | tf_op jit(solution)/shard_map/ppermute | solution.py:34
  282.9 0.1 add.92
  283.0 0.9 slice_multiply_fusion
  283.8 0.6 slice_multiply_fusion.1
  284.5 0.6 fusion.16
  (14 shorter events, 0.1 us)
Async XLA Ops:
  7.2 15.0 %copy-start = (bf16[512,1536]{1,0:T(8,128)(2,1)S(1)}, bf16[512,1536]{1,0:T(8,128)(2,1)}, u32[]{:S(2)}) copy-start(bf16[512,1536]{1,0:T(8,128)(2,1)} %param.7) | copy-start | bytes 4718596
  7.2 84.6 %all-gather.2.cloned.1.call-start = ((), (), s32[]{:S(2)}) async-start(), calls=%async_computation.1 | async-start | bytes 5013504 | tf_op jit(solution)/shard_map/all_gather | solution.py:43
  7.9 221.6 %reduce-scatter.2.cloned.1.call-start = ((), (), s32[]{:S(2)}) async-start(), calls=%async_computation.2 | async-start | bytes 10027008 | tf_op jit(solution)/shard_map/reduce_scatter | solution.py:59
  11.9 10.3 %copy-start.6 = (f32[1536]{0:T(1024)S(1)}, f32[1536]{0:T(1024)}, u32[]{:S(2)}) copy-start(f32[1536]{0:T(1024)} %param.10) | copy-start | bytes 18436
  20.5 1.7 copy-start.1
  27.7 71.3 %copy-start.5 = (bf16[512,1536]{1,0:T(8,128)(2,1)S(1)}, bf16[512,1536]{1,0:T(8,128)(2,1)}, u32[]{:S(2)}) copy-start(bf16[512,1536]{1,0:T(8,128)(2,1)} %param.6) | copy-start | bytes 4718596
  91.8 7.2 %copy-start.2 = (f32[512,1536]{1,0:T(8,128)S(1)}, f32[512,1536]{1,0:T(8,128)}, u32[]{:S(2)}) copy-start(f32[512,1536]{1,0:T(8,128)} %copy-done.1) | copy-start | bytes 9437188
  104.9 13.0 %collective-permute-start = (f32[6,1536]{1,0:T(8,128)S(1)}, f32[6,1536]{1,0:T(8,128)S(1)}, u32[]{:S(2)}, u32[]{:S(2)}) collective-permute-start(f32[6,1536]{1,0:T(8,128)S(1)} %concatenate.6), channel_id=1, source_target_pairs={{0,1},{1,0},{2,3},{3,2},{4,5},{5,4},{6,7},{7,6},{8,9},{9,8},{10,11... | collective-permute-start | bytes 110600 | tf_op jit(solution)/shard_map/ppermute | solution.py:34
  117.9 11.8 %collective-permute-start.1 = (f32[6,1536]{1,0:T(8,128)S(1)}, f32[6,1536]{1,0:T(8,128)S(1)}, u32[]{:S(2)}, u32[]{:S(2)}) collective-permute-start(f32[6,1536]{1,0:T(8,128)S(1)} %add.85), channel_id=1, source_target_pairs={{0,2},{1,3},{2,0},{3,1},{4,6},{5,7},{6,4},{7,5},{8,10},{9,11},{10,... | collective-permute-start | bytes 110600 | tf_op jit(solution)/shard_map/ppermute | solution.py:34
  129.7 5.1 %collective-permute-start.2 = (f32[6,1536]{1,0:T(8,128)S(1)}, f32[6,1536]{1,0:T(8,128)S(1)}, u32[]{:S(2)}, u32[]{:S(2)}) collective-permute-start(f32[6,1536]{1,0:T(8,128)S(1)} %add.86), channel_id=1, source_target_pairs={{0,4},{1,5},{2,6},{3,7},{4,0},{5,1},{6,2},{7,3},{8,12},{9,13},{10,... | collective-permute-start | bytes 110600 | tf_op jit(solution)/shard_map/ppermute | solution.py:34
  134.9 6.2 %collective-permute-start.3 = (f32[6,1536]{1,0:T(8,128)S(1)}, f32[6,1536]{1,0:T(8,128)S(1)}, u32[]{:S(2)}, u32[]{:S(2)}) collective-permute-start(f32[6,1536]{1,0:T(8,128)S(1)} %add.87), channel_id=1, source_target_pairs={{0,8},{1,9},{2,10},{3,11},{4,12},{5,13},{6,14},{7,15},{8,0},{9,1},... | collective-permute-start | bytes 110600 | tf_op jit(solution)/shard_map/ppermute | solution.py:34
  229.5 23.6 %copy-start.3 = (f32[512,1536]{1,0:T(8,128)S(1)}, f32[512,1536]{1,0:T(8,128)}, u32[]{:S(2)}) copy-start(f32[512,1536]{1,0:T(8,128)} %copy-done.1) | copy-start | bytes 9437188
  230.8 2.3 collective-permute-start.4
  234.3 16.5 %collective-permute-start.5 = (f32[102,1536]{1,0:T(8,128)S(1)}, f32[102,1536]{1,0:T(8,128)S(1)}, u32[]{:S(2)}, u32[]{:S(2)}) collective-permute-start(f32[102,1536]{1,0:T(8,128)S(1)} %fusion.25), channel_id=1, source_target_pairs={{0,32},{16,48},{32,0},{48,16},{64,96},{80,112},{96,64},{112,80},{1... | collective-permute-start | bytes 1880072 | tf_op jit(solution)/shard_map/ppermute | solution.py:34
  250.9 17.2 %collective-permute-start.6 = (f32[102,1536]{1,0:T(8,128)S(1)}, f32[102,1536]{1,0:T(8,128)S(1)}, u32[]{:S(2)}, u32[]{:S(2)}) collective-permute-start(f32[102,1536]{1,0:T(8,128)S(1)} %add.90), channel_id=1, source_target_pairs={{0,64},{16,80},{32,96},{48,112},{64,0},{80,16},{96,32},{112,48},{1... | collective-permute-start | bytes 1880072 | tf_op jit(solution)/shard_map/ppermute | solution.py:34
  253.1 16.1 %copy-start.4 = (f32[512,1536]{1,0:T(8,128)S(1)}, f32[512,1536]{1,0:T(8,128)}, u32[]{:S(2)}) copy-start(f32[512,1536]{1,0:T(8,128)} %get-tuple-element.18) | copy-start | bytes 9437188
  268.1 14.8 %collective-permute-start.7 = (f32[102,1536]{1,0:T(8,128)S(1)}, f32[102,1536]{1,0:T(8,128)S(1)}, u32[]{:S(2)}, u32[]{:S(2)}) collective-permute-start(f32[102,1536]{1,0:T(8,128)S(1)} %add.91), channel_id=1, source_target_pairs={{0,128},{16,144},{32,160},{48,176},{64,192},{80,208},{96,224},{112... | collective-permute-start | bytes 1880072 | tf_op jit(solution)/shard_map/ppermute | solution.py:34
Sparse Core Ops, SparseCore 0:
  10.5 81.2 all-gather.1
  95.6 133.8 reduce-scatter.1
where the time goes:
time: 292 us
  waiting for transfers between devices  214 us (73%)
  other arithmetic  25.9 us (9%)
  matrix products  19.6 us (7%)
  starting transfers between devices  15.1 us (5%)
  between operations  14.2 us (5%)
  local copies, waits for them, and re-layouts  3 us (1%)
    reduce_scatter x1, waiting for transfers between devices, shards(): lax.psum_scatter(weight_terms, 'fsdp', scatter_dimension=0, tiled=True)  88.5 us
    all_gather x1, waiting for transfers between devices, shards(): full_weight = lax.all_gather(out_weight, 'fsdp', axis=0, tiled=True)  64.1 us
    ppermute x8, waiting for transfers between devices, butterfly(): x = x + lax.ppermute(x, axis, pairs)  60.7 us
    ppermute x8, starting transfers between devices, butterfly(): x = x + lax.ppermute(x, axis, pairs)  15.1 us
    reduce_sum x1, other arithmetic, shards(): centred = mixed - jnp.mean(mixed, axis=-1, keepdims=True)  8.57 us
    dot_general x1, matrix products, shards(): lax.dot_general(grad_out, full_weight, (((1,), (1,)), ((), ())), preferre...  7.13 us
    dot_general x1, matrix products, shards(): jnp.dot(activation, full_weight, preferred_element_type=jnp.float32)  7.06 us
  transfers between devices with their start and end apart: 10, of which 10 were waited for; matrix products, arithmetic and copies ran while one was open for 15% of the time, Pallas kernels for 0%

commit v1 on v0

--- a/solution.py
+++ b/solution.py
@@ -3,6 +3,13 @@
 import jax.numpy as jnp
 from jax import lax
 from jax.sharding import PartitionSpec as P
+
+
+def write_indices(piece_in):
+    pile = []
+    for _ in range(lax.axis_size("fsdp")):
+        pile.append(piece_in)
+    return jnp.concatenate(lax.all_to_all(jnp.stack(pile), "fsdp", 0, 0), axis=0)
 
 
 def tap_mask(lengths, frames, count):
@@ -40,7 +47,7 @@
     frames, chans = hidden_in.shape
     count = conv_kernel.shape[0]
     half_width = count // 2
-    full_weight = lax.all_gather(out_weight, "fsdp", axis=0, tiled=True)
+    full_weight = write_indices(out_weight)
     taps = tap_mask(lengths[0], frames, count)
     live = taps[half_width][:, None]
     views = shifted(hidden_in, half_width)

time: 292 us -> 323 us (1.11)
  blocking collectives: 0 us -> 155 us
  waiting for transfers between devices: 214 us -> 89.1 us
  matrix products: 19.6 us -> 16.2 us
    all_to_all x0 -> x1, blocking collectives: none -> 155 us  [write_indices(): lax.all_to_all(jnp.stack(pile), 'fsdp', 0, 0)]
    all_gather x1 -> x0, waiting for transfers between devices: 64.1 us -> none  [shards(): full_weight = lax.all_gather(out_weight, 'fsdp', axis=0, tiled=True)]
    reduce_scatter x1, waiting for transfers between devices: 88.5 us -> 36.8 us  [shards(): lax.psum_scatter(weight_terms, 'fsdp', scatter_dimension=0, tiled=True)]
    ppermute x8, waiting for transfers between devices: 60.7 us -> 52.3 us  [butterfly(): x = x + lax.ppermute(x, axis, pairs)]
    dot_general x1, matrix products: 7.13 us -> 3.71 us  [shards(): lax.dot_general(grad_out, full_weight, (((1,), (1,)), ((), ())), preferre...]
  transfers between devices with their start and end apart: 10 -> 9, of which waited for: 10 -> 9; matrix products, arithmetic and copies ran while one was open for 15% -> 7% of each run, Pallas kernels for 0% -> 0%
where the time goes in v1:
time: 323 us; the launch traced here: 322 us
  blocking collectives  155 us (48%)
  waiting for transfers between devices  89.1 us (28%)
  other arithmetic  25.4 us (8%)
  starting transfers between devices  17.7 us (5%)
  matrix products  16.2 us (5%)
  between operations  14.2 us (4%)
  local copies, waits for them, and re-layouts  4.39 us (1%)
    all_to_all x1, blocking collectives, write_indices(): lax.all_to_all(jnp.stack(pile), 'fsdp', 0, 0)  155 us
    ppermute x8, waiting for transfers between devices, butterfly(): x = x + lax.ppermute(x, axis, pairs)  52.3 us
    reduce_scatter x1, waiting for transfers between devices, shards(): lax.psum_scatter(weight_terms, 'fsdp', scatter_dimension=0, tiled=True)  36.8 us
    ppermute x8, starting transfers between devices, butterfly(): x = x + lax.ppermute(x, axis, pairs)  17.7 us
    reduce_sum x1, other arithmetic, shards(): centred = mixed - jnp.mean(mixed, axis=-1, keepdims=True)  8.57 us
    dot_general x1, matrix products, shards(): jnp.dot(activation, full_weight, preferred_element_type=jnp.float32)  7.11 us
  transfers between devices with their start and end apart: 9, of which 9 were waited for; matrix products, arithmetic and copies ran while one was open for 7% of the time, Pallas kernels for 0%

profile of v1, /device:TPU:2, one launch (start us, length us, event | category | flops | bytes accessed | tf_op | source)
XLA Modules:
  0.0 322.5 jit_solution(12618182744964249653)
XLA Ops:
  7.2 0.0 copy-start
  7.2 0.0 reduce-scatter.2.cloned.1.call-start
  7.2 0.9 reduce-window.4
  8.2 0.6 slice.88
  8.7 0.6 iota_compare_fusion.1
  9.4 0.1 convert_reduce_fusion
  9.5 1.1 slice_reduce_fusion.4
  10.6 0.1 and_convert_fusion.4
  10.7 0.0 copy-start.8
  10.7 8.6 %fusion.28 = (f32[512]{0:T(512)S(1)}, f32[512,1536]{1,0:T(8,128)S(1)}) fusion(f32[512]{0:T(512)S(1)} %get-tuple-element.24, f32[1536]{0:T(1024)S(1)} %get-tuple-element.16, f32[512]{0:T(512)S(1)} %get-tuple-element.22, f32[1536]{0:T(1024)S(1)} %get-tuple-element.17, f32[512]{0:T(512)S(1)} %get-tuple-element.27, bf16[512,1536]{1,0:T(8,128)(2,1)} %param.6, ...), kind=kLoop, calls=%fused_computation.80 | loop fusion | flops 15728128 | bytes 4761600 | tf_op jit(solution)/shard_map/reduce_sum | solution.py:57
  19.2 0.0 copy-start.1
  19.3 0.4 multiply_reduce_fusion.2
  19.7 1.2 copy-done.1
  20.9 0.0 copy-done
  20.9 0.0 copy-done.8
  20.9 5.4 %fusion.26 = f32[1536,1536]{1,0:T(8,128)} fusion(bf16[512,1536]{1,0:T(8,128)(2,1)S(1)} %copy-done, f32[512,1536]{1,0:T(8,128)S(1)} %get-tuple-element.20, f32[1536]{0:T(1024)S(1)} %copy-done.8, f32[512]{0:T(512)S(1)} %add_rsqrt_fusion, f32[512]{0:T(512)S(1)} %broadcast_multiply_fusion.2, f32[512]{0:T(512)S(1)} %get-tuple-element.27), kind=kOutput, calls=%fused_computation.78 | convolution fusion | flops 2422996992 | bytes 14168064 | tf_op jit(solution)/shard_map/dot_general | solution.py:63
  26.3 0.0 copy-start.7
  26.3 0.0 reduce-scatter.2.cloned.1.call-update
  26.4 0.9 copy-done.7
  27.3 0.4 stack.12
  27.7 0.0 copy-start.2
  27.8 155.5 %all_to_all.5 = bf16[16,96,1536]{2,1,0:T(8,128)(2,1)S(1)} all-to-all(bf16[16,96,1536]{2,1,0:T(8,128)(2,1)S(1)} %stack.12), channel_id=1, replica_groups=mesh['dp'=16,'fsdp'=16] {'fsdp'}, dimensions={0} | all-to-all | bytes 9437184 | tf_op jit(solution)/shard_map/all_to_all | solution.py:12
  183.2 0.0 copy-start.6
  183.2 0.0 copy-done.2
  183.2 0.0 copy-start.5
  183.2 3.7 %multiply_reduce_fusion = (f32[1536]{0:T(1024)S(1)}, f32[512]{0:T(512)S(1)}, f32[512]{0:T(512)S(1)}, f32[512,1536]{1,0:T(8,128)S(1)}) fusion(f32[512,1536]{1,0:T(8,128)S(1)} %copy-done.2, f32[512]{0:T(512)S(1)} %add_rsqrt_fusion, f32[512]{0:T(512)S(1)} %broadcast_multiply_fusion.2, f32[1536]{0:T(1024)S(1)} %copy-done.8, f32[512]{0:T(512)S(1)} %get-tuple-element.27, ...), kind=kOutput, calls=%fused_computation.27 | convolution fusion | flops 2430072320 | bytes 12605440 | tf_op jit(solution)/shard_map/dot_general | solution.py:68
  186.9 0.0 copy-done.6
  187.0 0.0 copy-done.5
  187.0 5.8 %fusion.15 = (f32[1536]{0:T(1024)S(1)}, f32[1536]{0:T(1024)S(1)}, f32[1536]{0:T(1024)S(1)}, f32[1536]{0:T(1024)S(1)}, f32[1536]{0:T(1024)S(1)}, /*index=5*/f32[512,1536]{1,0:T(8,128)}) fusion(f32[512]{0:T(512)S(1)} %get-tuple-element.24, bf16[512,1536]{1,0:T(8,128)(2,1)S(1)} %copy-done.5, f32[512]{0:T(512)S(1)} %get-tuple-element.22, ...), kind=kLoop, calls=%fused_computation.26 | loop fusion | flops 21225984 | bytes 11065344 | tf_op jit(solution)/shard_map/reduce_sum | solution.py:82
  192.8 0.1 concatenate.6
  192.9 2.5 collective-permute-start
  195.4 4.6 %collective-permute-done = f32[6,1536]{1,0:T(8,128)S(1)} collective-permute-done((f32[6,1536]{1,0:T(8,128)S(1)}, f32[6,1536]{1,0:T(8,128)S(1)}, u32[]{:S(2)}, u32[]{:S(2)}) %collective-permute-start) | collective-permute-done | bytes 36896 | tf_op jit(solution)/shard_map/ppermute | solution.py:41
  200.0 3.0 collective-permute-start.1
  203.0 7.5 %collective-permute-done.1 = f32[6,1536]{1,0:T(8,128)S(1)} collective-permute-done((f32[6,1536]{1,0:T(8,128)S(1)}, f32[6,1536]{1,0:T(8,128)S(1)}, u32[]{:S(2)}, u32[]{:S(2)}) %collective-permute-start.1) | collective-permute-done | bytes 36896 | tf_op jit(solution)/shard_map/ppermute | solution.py:41
  210.5 3.3 %collective-permute-start.2 = (f32[6,1536]{1,0:T(8,128)S(1)}, f32[6,1536]{1,0:T(8,128)S(1)}, u32[]{:S(2)}, u32[]{:S(2)}) collective-permute-start(f32[6,1536]{1,0:T(8,128)S(1)} %add.86), channel_id=1, source_target_pairs={{0,4},{1,5},{2,6},{3,7},{4,0},{5,1},{6,2},{7,3},{8,12},{9,13},{10,... | collective-permute-start | bytes 110600 | tf_op jit(solution)/shard_map/ppermute | solution.py:41
  213.8 2.4 collective-permute-done.2
  216.2 4.9 %collective-permute-start.3 = (f32[6,1536]{1,0:T(8,128)S(1)}, f32[6,1536]{1,0:T(8,128)S(1)}, u32[]{:S(2)}, u32[]{:S(2)}) collective-permute-start(f32[6,1536]{1,0:T(8,128)S(1)} %add.87), channel_id=1, source_target_pairs={{0,8},{1,9},{2,10},{3,11},{4,12},{5,13},{6,14},{7,15},{8,0},{9,1},... | collective-permute-start | bytes 110600 | tf_op jit(solution)/shard_map/ppermute | solution.py:41
  221.1 2.4 collective-permute-done.3
  223.5 36.8 %reduce-scatter.2.cloned.1.call-done = f32[96,1536]{1,0:T(8,128)} async-done(((f32[1536,1536]{1,0:T(8,128)}), f32[96,1536]{1,0:T(8,128)}) %reduce-scatter.2.cloned.1.call-update) | async-done | bytes 589840 | tf_op jit(solution)/shard_map/reduce_scatter | solution.py:66
  260.3 0.0 copy-start.3
  260.3 1.3 pad_maximum_fusion
  261.5 0.1 collective-permute-start.4
  261.6 2.1 collective-permute-done.4
  263.7 1.1 fusion.25
  264.8 0.5 collective-permute-start.5
  265.4 16.0 %collective-permute-done.5 = f32[102,1536]{1,0:T(8,128)S(1)} collective-permute-done((f32[102,1536]{1,0:T(8,128)S(1)}, f32[102,1536]{1,0:T(8,128)S(1)}, u32[]{:S(2)}, u32[]{:S(2)}) %collective-permute-start.5) | collective-permute-done | bytes 626720 | tf_op jit(solution)/shard_map/ppermute | solution.py:41
  281.3 0.1 add.90
  281.4 2.1 collective-permute-start.6
  283.5 0.0 copy-done.3
  283.5 0.0 copy-start.4
  283.6 7.1 %fusion.27 = f32[512,1536]{1,0:T(8,128)} fusion(bf16[1536,1536]{1,0:T(8,128)(2,1)} %bitcast.9, f32[512,1536]{1,0:T(8,128)S(1)} %copy-done.3, f32[1536]{0:T(1024)S(1)} %copy-done.8, f32[512]{0:T(512)S(1)} %add_rsqrt_fusion, f32[512]{0:T(512)S(1)} %broadcast_multiply_fusion.2, f32[512]{0:T(512)S(1)} %get-tuple-element.27), kind=kOutput, calls=%fused_computation.79 | convolution fusion | flops 2422996992 | bytes 11022336 | tf_op jit(solution)/shard_map/dot_general | solution.py:67
  290.7 7.9 %collective-permute-done.6 = f32[102,1536]{1,0:T(8,128)S(1)} collective-permute-done((f32[102,1536]{1,0:T(8,128)S(1)}, f32[102,1536]{1,0:T(8,128)S(1)}, u32[]{:S(2)}, u32[]{:S(2)}) %collective-permute-start.6) | collective-permute-done | bytes 626720 | tf_op jit(solution)/shard_map/ppermute | solution.py:41
  298.6 0.1 add.91
  298.7 1.2 collective-permute-start.7
  299.8 0.0 copy-done.4
  299.9 4.1 %multiply_add_fusion = f32[512,1536]{1,0:T(8,128)} fusion(f32[512,1536]{1,0:T(8,128)S(1)} %copy-done.4, f32[512]{0:T(512)S(1)} %get-tuple-element.24, f32[1536]{0:T(1024)S(1)} %get-tuple-element.16, f32[512]{0:T(512)S(1)} %get-tuple-element.22, f32[1536]{0:T(1024)S(1)} %get-tuple-element.17, f32[512]{0:T(512)S(1)} %get-tuple-element.27, ...), kind=kLoop, calls=%fused_computation.28 | loop fusion | flops 11010048 | bytes 6332416 | tf_op jit(solution)/shard_map/add | solution.py:86
  303.9 9.5 %collective-permute-done.7 = f32[102,1536]{1,0:T(8,128)S(1)} collective-permute-done((f32[102,1536]{1,0:T(8,128)S(1)}, f32[102,1536]{1,0:T(8,128)S(1)}, u32[]{:S(2)}, u32[]{:S(2)}) %collective-permute-start.7) | collective-permute-done | bytes 626720 | tf_op jit(solution)/shard_map/ppermute | solution.py:41
  313.5 0.1 add.92
  313.5 0.9 slice_multiply_fusion
  314.4 0.6 slice_multiply_fusion.1
  315.0 0.6 fusion.16
  (14 shorter events, 0.1 us)
Async XLA Ops:
  7.2 13.7 %copy-start = (bf16[512,1536]{1,0:T(8,128)(2,1)S(1)}, bf16[512,1536]{1,0:T(8,128)(2,1)}, u32[]{:S(2)}) copy-start(bf16[512,1536]{1,0:T(8,128)(2,1)} %param.7) | copy-start | bytes 4718596
  7.2 253.1 %reduce-scatter.2.cloned.1.call-start = ((), (), s32[]{:S(2)}) async-start(), calls=%async_computation.2 | async-start | bytes 10027008 | tf_op jit(solution)/shard_map/reduce_scatter | solution.py:66
  10.7 10.2 %copy-start.8 = (f32[1536]{0:T(1024)S(1)}, f32[1536]{0:T(1024)}, u32[]{:S(2)}) copy-start(f32[1536]{0:T(1024)} %param.10) | copy-start | bytes 18436
  19.2 1.7 copy-start.1
  26.3 1.0 copy-start.7
  27.7 155.5 %copy-start.2 = (f32[512,1536]{1,0:T(8,128)S(1)}, f32[512,1536]{1,0:T(8,128)}, u32[]{:S(2)}) copy-start(f32[512,1536]{1,0:T(8,128)} %copy-done.1) | copy-start | bytes 9437188
  183.2 3.7 %copy-start.6 = (bf16[16,96,1536]{2,1,0:T(8,128)(2,1)}, bf16[16,96,1536]{2,1,0:T(8,128)(2,1)S(1)}, u32[]{:S(2)}) copy-start(bf16[16,96,1536]{2,1,0:T(8,128)(2,1)S(1)} %all_to_all.5) | copy-start | bytes 14155780
  183.2 3.7 %copy-start.5 = (bf16[512,1536]{1,0:T(8,128)(2,1)S(1)}, bf16[512,1536]{1,0:T(8,128)(2,1)}, u32[]{:S(2)}) copy-start(bf16[512,1536]{1,0:T(8,128)(2,1)} %param.6) | copy-start | bytes 4718596
  192.9 7.1 %collective-permute-start = (f32[6,1536]{1,0:T(8,128)S(1)}, f32[6,1536]{1,0:T(8,128)S(1)}, u32[]{:S(2)}, u32[]{:S(2)}) collective-permute-start(f32[6,1536]{1,0:T(8,128)S(1)} %concatenate.6), channel_id=1, source_target_pairs={{0,1},{1,0},{2,3},{3,2},{4,5},{5,4},{6,7},{7,6},{8,9},{9,8},{10,11... | collective-permute-start | bytes 110600 | tf_op jit(solution)/shard_map/ppermute | solution.py:41
  200.0 10.5 %collective-permute-start.1 = (f32[6,1536]{1,0:T(8,128)S(1)}, f32[6,1536]{1,0:T(8,128)S(1)}, u32[]{:S(2)}, u32[]{:S(2)}) collective-permute-start(f32[6,1536]{1,0:T(8,128)S(1)} %add.85), channel_id=1, source_target_pairs={{0,2},{1,3},{2,0},{3,1},{4,6},{5,7},{6,4},{7,5},{8,10},{9,11},{10,... | collective-permute-start | bytes 110600 | tf_op jit(solution)/shard_map/ppermute | solution.py:41
  210.5 5.7 %collective-permute-start.2 = (f32[6,1536]{1,0:T(8,128)S(1)}, f32[6,1536]{1,0:T(8,128)S(1)}, u32[]{:S(2)}, u32[]{:S(2)}) collective-permute-start(f32[6,1536]{1,0:T(8,128)S(1)} %add.86), channel_id=1, source_target_pairs={{0,4},{1,5},{2,6},{3,7},{4,0},{5,1},{6,2},{7,3},{8,12},{9,13},{10,... | collective-permute-start | bytes 110600 | tf_op jit(solution)/shard_map/ppermute | solution.py:41
  216.2 7.3 %collective-permute-start.3 = (f32[6,1536]{1,0:T(8,128)S(1)}, f32[6,1536]{1,0:T(8,128)S(1)}, u32[]{:S(2)}, u32[]{:S(2)}) collective-permute-start(f32[6,1536]{1,0:T(8,128)S(1)} %add.87), channel_id=1, source_target_pairs={{0,8},{1,9},{2,10},{3,11},{4,12},{5,13},{6,14},{7,15},{8,0},{9,1},... | collective-permute-start | bytes 110600 | tf_op jit(solution)/shard_map/ppermute | solution.py:41
  260.3 23.3 %copy-start.3 = (f32[512,1536]{1,0:T(8,128)S(1)}, f32[512,1536]{1,0:T(8,128)}, u32[]{:S(2)}) copy-start(f32[512,1536]{1,0:T(8,128)} %copy-done.1) | copy-start | bytes 9437188
  261.5 2.2 collective-permute-start.4
  264.8 16.5 %collective-permute-start.5 = (f32[102,1536]{1,0:T(8,128)S(1)}, f32[102,1536]{1,0:T(8,128)S(1)}, u32[]{:S(2)}, u32[]{:S(2)}) collective-permute-start(f32[102,1536]{1,0:T(8,128)S(1)} %fusion.25), channel_id=1, source_target_pairs={{0,32},{16,48},{32,0},{48,16},{64,96},{80,112},{96,64},{112,80},{1... | collective-permute-start | bytes 1880072 | tf_op jit(solution)/shard_map/ppermute | solution.py:41
  281.4 17.2 %collective-permute-start.6 = (f32[102,1536]{1,0:T(8,128)S(1)}, f32[102,1536]{1,0:T(8,128)S(1)}, u32[]{:S(2)}, u32[]{:S(2)}) collective-permute-start(f32[102,1536]{1,0:T(8,128)S(1)} %add.90), channel_id=1, source_target_pairs={{0,64},{16,80},{32,96},{48,112},{64,0},{80,16},{96,32},{112,48},{1... | collective-permute-start | bytes 1880072 | tf_op jit(solution)/shard_map/ppermute | solution.py:41
  283.5 16.3 %copy-start.4 = (f32[512,1536]{1,0:T(8,128)S(1)}, f32[512,1536]{1,0:T(8,128)}, u32[]{:S(2)}) copy-start(f32[512,1536]{1,0:T(8,128)} %get-tuple-element.18) | copy-start | bytes 9437188
  298.7 14.8 %collective-permute-start.7 = (f32[102,1536]{1,0:T(8,128)S(1)}, f32[102,1536]{1,0:T(8,128)S(1)}, u32[]{:S(2)}, u32[]{:S(2)}) collective-permute-start(f32[102,1536]{1,0:T(8,128)S(1)} %add.91), channel_id=1, source_target_pairs={{0,128},{16,144},{32,160},{48,176},{64,192},{80,208},{96,224},{112... | collective-permute-start | bytes 1880072 | tf_op jit(solution)/shard_map/ppermute | solution.py:41
Sparse Core Ops, SparseCore 0:
  26.5 233.7 reduce-scatter.1
